TPU v7x, 32 devices: a whole 2x2x4 slice. The times are simulated.
32 devices in a mesh: grp: 4 (over z), exp: 8 (over y, x, core).
Axes of the slice: x: 2, y: 2, z: 4, core: 2. Of those that a mesh axis runs over, the one named last changes fastest.
Arguments:
- cotangent: bfloat16 [4096, 1440], P(('grp', 'exp')), may hold values from -6 to 6
- hidden: bfloat16 [4096, 4, 1440], P(('grp', 'exp')), may hold values from -0.29882812 to 0.29882812
- gates: bfloat16 [4096, 4], P(('grp', 'exp')), may hold values from 0.049804688 to 1
- expert_ids: int32 [4096, 4], P(('grp', 'exp')), may hold values from 0 to 15, all different within a row; in each aligned block of 128 rows (0 to 127, 128 to 255, ...) at most 40 rows name the same one
- group_counts: int32 [4], P('grp'), may hold values from 146 to 1024, as said below
- w_down: bfloat16 [16, 1440, 1440], P('exp', 'grp'), may hold values from -0.15625 to 0.15625
Outputs:
- d_hidden: bfloat16 [4096, 4, 1440], P(('grp', 'exp'))
- d_gate: bfloat16 [4096, 4], P(('grp', 'exp'))
- d_weight: float32 [16, 1440, 1440], P('exp', 'grp')
Inputs may be any that keep to these rules, and one draw needn't show every extreme that they name: `expert_ids`: within the rows of one device no expert is named more than 40 times, and every expert is named somewhere. `group_counts`: some group has all 1024 slots live, and some group only 146.
All inputs are finite; a program needn't handle non-finite values.
Results may differ from a plain program's by a relative error of at most 0.015.
Values may be sent and summed in bfloat16 or wider, within the bound.
No kernel may reach another device: no remote copies, remote signals or barrier semaphores. Data moves between devices by JAX's collectives and lax.ppermute only.
A program may use at most 128 MiB of HBM per device.

v0:
```python
import jax
import jax.numpy as jnp
from jax import lax
from jax.sharding import PartitionSpec as P

LOSS_SCALE = 32768


def body(cotangent, hidden, gates, expert_ids, group_counts, w_down):
    tok = cotangent.shape[0]
    top = expert_ids.shape[1]
    ffw = hidden.shape[2]
    width = cotangent.shape[1]
    n_exp = lax.axis_size("exp")
    exp_dev = w_down.shape[0]
    experts = exp_dev * n_exp
    most = 5 * tok * top // (4 * experts)
    count = group_counts[0]
    first_row = lax.axis_index("exp") * tok
    live = (first_row + jnp.arange(tok, dtype=jnp.int32) < count).astype(jnp.float32)
    total = lax.psum(count.astype(jnp.float32), "grp")
    scale = LOSS_SCALE / total
    weighted = (gates.astype(jnp.float32) * live[:, None]).astype(jnp.bfloat16)
    flat_ids = expert_ids.reshape(-1)
    onehot = (flat_ids[:, None] == jnp.arange(experts, dtype=jnp.int32)[None, :]).astype(jnp.int32)
    rank = jnp.sum((jnp.cumsum(onehot, axis=0) - onehot) * onehot, axis=1)
    target = flat_ids * most + rank
    slot_tok = jnp.arange(tok * top, dtype=jnp.int32) // top
    dy_buf = jnp.zeros((experts * most, width), jnp.bfloat16).at[target].set(cotangent[slot_tok])
    hid_buf = jnp.zeros((experts * most, ffw), jnp.bfloat16).at[target].set(hidden.reshape(-1, ffw))
    gate_buf = jnp.zeros((experts * most,), jnp.bfloat16).at[target].set(weighted.reshape(-1))
    dy_buf = dy_buf.reshape(n_exp, exp_dev * most, width)
    hid_buf = hid_buf.reshape(n_exp, exp_dev * most, ffw)
    gate_buf = gate_buf.reshape(n_exp, exp_dev * most)
    dy_recv, gate_recv = (
        lax.all_to_all(dy_buf, "exp", split_axis=0, concat_axis=0, tiled=True),
        lax.all_to_all(gate_buf, "exp", split_axis=0, concat_axis=0, tiled=True),
    )
    hid_recv = lax.all_to_all(hid_buf, "exp", split_axis=0, concat_axis=0, tiled=True)
    dy_four = dy_recv.reshape(n_exp, exp_dev, most, width)
    hid_four = hid_recv.reshape(n_exp, exp_dev, most, ffw)
    gate_three = gate_recv.reshape(n_exp, exp_dev, most).astype(jnp.float32)
    proj = jnp.einsum(
        "sjmd,jfd->sjmf",
        dy_four,
        lax.all_gather(w_down, "grp", axis=1, tiled=True),
        preferred_element_type=jnp.float32,
    )
    dh_rows = (gate_three[..., None] * proj).astype(jnp.bfloat16)
    inner = jnp.sum(hid_four.astype(jnp.float32) * proj, axis=3).astype(jnp.bfloat16)
    scaled = (gate_three[..., None] * dy_four.astype(jnp.float32)).astype(jnp.bfloat16)
    partial_grad = (
        jnp.einsum("sjmf,sjmd->jfd", hid_four, scaled, preferred_element_type=jnp.float32) * scale
    )
    d_weight = lax.psum_scatter(
        partial_grad.astype(jnp.bfloat16), "grp", scatter_dimension=1, tiled=True
    ).astype(jnp.float32)
    back_dh, back_inner = (
        lax.all_to_all(
            dh_rows.reshape(n_exp, exp_dev * most, ffw),
            "exp",
            split_axis=0,
            concat_axis=0,
            tiled=True,
        ),
        lax.all_to_all(
            inner.reshape(n_exp, exp_dev * most), "exp", split_axis=0, concat_axis=0, tiled=True
        ),
    )
    d_hidden = back_dh.reshape(experts * most, ffw)[target].reshape(tok, top, ffw)
    inner_tok = back_inner.reshape(-1)[target].reshape(tok, top)
    d_gate = (inner_tok.astype(jnp.float32) * live[:, None]).astype(jnp.bfloat16)
    return (d_hidden, d_gate, d_weight)


def solution(mesh):
    in_specs = (
        P(("grp", "exp"), None),
        P(("grp", "exp"), None, None),
        P(("grp", "exp"), None),
        P(("grp", "exp"), None),
        P("grp"),
        P("exp", "grp", None),
    )
    out_specs = (P(("grp", "exp"), None, None), P(("grp", "exp"), None), P("exp", "grp", None))
    return jax.shard_map(body, mesh=mesh, in_specs=in_specs, out_specs=out_specs, check_vma=False)
```

profile of v0, /device:TPU:0, one launch (start us, length us, event | category | flops | bytes accessed | tf_op | source)
XLA Modules:
  0.0 501.5 jit_solution(16202728035999669125)
XLA Ops:
  7.2 0.7 all-gather.2.cloned.1.call-update
  8.5 1.2 reduce-window.6
  9.7 0.2 slice_reduce_fusion
  11.0 3.8 scatter_custom_fusion
  14.8 0.7 all_to_all.25
  15.5 5.2 %all-to-all-start = ((bf16[8,1,80]{2,1,0:T(2,128)(2,1)}), bf16[8,1,80]{2,1,0:T(2,128)(2,1)S(1)}, u32[]{:S(2)}, u32[]{:S(2)}) async-start(bf16[8,1,80]{2,1,0:T(2,128)(2,1)} %all_to_all.25), calls=%async_computation | async-start | bytes 8192 | tf_op jit(solution)/shard_map/all_to_all | solution.py:37
  20.6 1.6 copy.55
  22.2 0.8 reshape.220
  23.0 4.5 scatter_custom_fusion.2
  27.5 4.3 all-to-all-start.3
  32.0 9.6 %scatter_custom_fusion.1 = bf16[640,1440]{1,0:T(8,128)(2,1)} fusion(s32[512]{0:T(512)S(1)} %bitcast.59, bf16[128,1440]{1,0:T(8,128)(2,1)S(1)} %copy.52, s32[1024]{0:T(1024)S(1)} %pad_clamp_fusion.1, bf16[]{:T(256)} %constant.15.clone.1), kind=kCustom, calls=%fused_computation.18 | custom fusion | bytes 1843202 | tf_op jit(solution)/shard_map/scatter | solution.py:29
  41.6 15.5 %all-to-all-done.3 = bf16[8,80,1440]{2,1,0:T(8,128)(2,1)S(1)} async-done(((bf16[8,80,1440]{2,1,0:T(8,128)(2,1)}), bf16[8,80,1440]{2,1,0:T(8,128)(2,1)S(1)}, u32[]{:S(2)}, u32[]{:S(2)}) %all-to-all-start.3) | async-done | bytes 1843232 | tf_op jit(solution)/shard_map/all_to_all | solution.py:39
  57.0 4.3 all-to-all-start.1
  61.4 15.4 %psum.7 = f32[]{:T(128)} all-reduce(f32[]{:T(128)S(6)} %convert_element_type.90), channel_id=1, replica_groups=mesh['grp'=4,'exp'=8] {'grp'}, use_global_device_ids=true, to_apply=%region_7.8 | all-reduce | flops 1 | bytes 8 | tf_op jit(solution)/shard_map/psum | solution.py:21
  77.6 9.0 %all-to-all-done.1 = bf16[8,80,1440]{2,1,0:T(8,128)(2,1)} async-done(((bf16[8,80,1440]{2,1,0:T(8,128)(2,1)}), bf16[8,80,1440]{2,1,0:T(8,128)(2,1)}, u32[]{:S(2)}, u32[]{:S(2)}) %all-to-all-start.1) | async-done | bytes 1843232 | tf_op jit(solution)/shard_map/all_to_all | solution.py:36
  86.6 83.1 %all-gather.2.cloned.1.call-done = bf16[2,1440,1440]{2,1,0:T(8,128)(2,1)} async-done(((bf16[2,360,1440]{2,1,0:T(8,128)(2,1)}), bf16[2,1440,1440]{2,1,0:T(8,128)(2,1)}) %all-gather.2.cloned.1.call-update) | async-done | bytes 8294416 | tf_op jit(solution)/shard_map/all_gather | solution.py:46
  169.7 9.6 %fusion.4 = (bf16[8,2,40]{2,0,1:T(8,128)(2,1)S(1)}, bf16[8,2,40,1440]{3,2,0,1:T(8,128)(2,1)}, bf16[8,2,40,1440]{3,2,0,1:T(8,128)(2,1)S(1)}) fusion(bf16[8,2,40,1440]{3,2,1,0:T(8,128)(2,1)S(1)} %bitcast.55, f32[8,2,40]{2,0,1:T(8,128)S(1)} %copy.51, bf16[8,2,40,1440]{3,2,1,0:T(8,128)(2,1)} %bitcast.6, bf16[2,1440,1440]{2,1,0:T(8,128)(2,1)} %all-gather.2.cloned.1.call-done), kind=kOutput, calls=%fused_computation.13 | convolution fusion | flops 2661580288 | bytes 15671040 | tf_op jit(solution)/shard_map/sjmd,jfd->sjmf/dot_general | solution.py:43
  179.3 7.1 %fusion = bf16[2,1440,1440]{2,1,0:T(8,128)(2,1)} fusion(bf16[8,2,40,1440]{3,2,1,0:T(8,128)(2,1)S(1)} %bitcast.56, f32[]{:T(128)S(6)} %div.13, bf16[8,2,40,1440]{3,2,0,1:T(8,128)(2,1)S(1)} %get-tuple-element.17), kind=kOutput, calls=%fused_computation.7 | convolution fusion | flops 2662502400 | bytes 11980804 | tf_op jit(solution)/shard_map/sjmf,sjmd->jfd/dot_general | solution.py:53
  186.4 0.7 convert_element_type.95
  187.0 3.7 all-to-all-start.4
  190.7 1.5 copy.54
  192.1 3.1 all-to-all-done.4
  195.3 3.7 all-to-all-start.2
  199.0 0.6 dynamic-slice
  200.4 3.5 gather_fusion.1
  204.1 0.7 copy.62
  204.8 19.4 %all-to-all-done.2 = bf16[8,80,1440]{2,1,0:T(8,128)(2,1)S(1)} async-done(((bf16[8,80,1440]{2,1,0:T(8,128)(2,1)}), bf16[8,80,1440]{2,1,0:T(8,128)(2,1)S(1)}, u32[]{:S(2)}, u32[]{:S(2)}) %all-to-all-start.2) | async-done | bytes 1843232 | tf_op jit(solution)/shard_map/all_to_all | solution.py:59
  224.2 2.1 gather_fusion
  226.3 0.4 reshape.169
  226.7 2.4 copy.61
  229.2 261.2 %all-reduce.3.cloned.1.call-done = bf16[2,1440,1440]{2,1,0:T(8,128)(2,1)} async-done(((bf16[2,1440,1440]{2,1,0:T(8,128)(2,1)}), bf16[2,1440,1440]{2,1,0:T(8,128)(2,1)}) %all-reduce.3.cloned.1.call-update) | async-done | bytes 8294416
  490.3 4.3 dynamic-slice_convert_fusion
  (43 shorter events, 1.7 us)
Async XLA Ops:
  7.2 0.8 copy-start.3
  7.2 3.4 copy-start.4
  7.2 13.4 %copy-start.1 = (bf16[128,4,1440]{0,2,1:T(8,128)(2,1)S(1)}, bf16[128,4,1440]{0,2,1:T(8,128)(2,1)}, u32[]{:S(2)}) copy-start(bf16[128,4,1440]{0,2,1:T(8,128)(2,1)} %param.7) | copy-start | bytes 4423684
  7.2 162.5 %all-gather.2.cloned.1.call-start = ((), (), s32[]{:S(2)}) async-start(), calls=%async_computation.5 | async-start | bytes 11059200 | tf_op jit(solution)/shard_map/all_gather | solution.py:46
  15.5 12.0 %all-to-all-start = ((bf16[8,1,80]{2,1,0:T(2,128)(2,1)}), bf16[8,1,80]{2,1,0:T(2,128)(2,1)S(1)}, u32[]{:S(2)}, u32[]{:S(2)}) async-start(bf16[8,1,80]{2,1,0:T(2,128)(2,1)} %all_to_all.25), calls=%async_computation | async-start | bytes 8192 | tf_op jit(solution)/shard_map/all_to_all | solution.py:37
  27.5 4.3 copy-start.2
  27.5 29.6 %all-to-all-start.3 = ((bf16[8,80,1440]{2,1,0:T(8,128)(2,1)}), bf16[8,80,1440]{2,1,0:T(8,128)(2,1)S(1)}, u32[]{:S(2)}, u32[]{:S(2)}) async-start(bf16[8,80,1440]{2,1,0:T(8,128)(2,1)} %bitcast.12), calls=%async_computation.3 | async-start | bytes 3932160 | tf_op jit(solution)/shard_map/all_to_all | solution.py:39
  57.0 29.6 %all-to-all-start.1 = ((bf16[8,80,1440]{2,1,0:T(8,128)(2,1)}), bf16[8,80,1440]{2,1,0:T(8,128)(2,1)}, u32[]{:S(2)}, u32[]{:S(2)}) async-start(bf16[8,80,1440]{2,1,0:T(8,128)(2,1)} %bitcast.5), calls=%async_computation.1 | async-start | bytes 3932160 | tf_op jit(solution)/shard_map/all_to_all | solution.py:36
  61.4 429.0 %all-reduce.3.cloned.1.call-start = ((), (), s32[]{:S(2)}) async-start(), calls=%async_computation.6 | async-start | bytes 17694720
  186.3 4.4 copy-start
  187.0 8.2 %all-to-all-start.4 = ((bf16[8,1,80]{2,1,0:T(2,128)(2,1)}), bf16[8,1,80]{2,1,0:T(2,128)(2,1)S(1)}, u32[]{:S(2)}, u32[]{:S(2)}) async-start(bf16[8,1,80]{2,1,0:T(2,128)(2,1)} %convert_element_type.95), calls=%async_computation.4 | async-start | bytes 8192 | tf_op jit(solution)/shard_map/all_to_all | solution.py:66
  195.3 3.7 copy-start.5
  195.3 28.9 %all-to-all-start.2 = ((bf16[8,80,1440]{2,1,0:T(8,128)(2,1)}), bf16[8,80,1440]{2,1,0:T(8,128)(2,1)S(1)}, u32[]{:S(2)}, u32[]{:S(2)}) async-start(bf16[8,80,1440]{2,1,0:T(8,128)(2,1)} %bitcast.54), calls=%async_computation.2 | async-start | bytes 3932160 | tf_op jit(solution)/shard_map/all_to_all | solution.py:59
Sparse Core Ops, SparseCore 0:
  9.6 160.0 all-gather.1
  186.5 303.8 all-reduce.2
where the time goes:
time: 502 us; the launch traced here: 501 us
  waiting for transfers between devices  392 us (78%)
  local copies, waits for them, and re-layouts  34.2 us (7%)
  starting transfers between devices  21.3 us (4%)
  matrix products  16.6 us (3%)
  between operations  16.3 us (3%)
  blocking collectives  15.4 us (3%)
  other arithmetic  5.77 us (1%)
    unnamed x3, waiting for transfers between devices  262 us
    all_gather x1, waiting for transfers between devices, body(): lax.all_gather(w_down, 'grp', axis=1, tiled=True)  83.1 us
    all_to_all x1, waiting for transfers between devices, body(): lax.all_to_all(dh_rows.reshape(n_exp, exp_dev * most, ffw), 'exp', split_...  19.4 us
    all_to_all x1, waiting for transfers between devices, body(): lax.all_to_all(hid_buf, 'exp', split_axis=0, concat_axis=0, tiled=True)  15.5 us
    psum x1, blocking collectives, body(): total = lax.psum(count.astype(jnp.float32), 'grp')  15.4 us
  transfers between devices with their start and end apart: 7, of which 6 were waited for; matrix products, arithmetic and copies ran while one was open for 7% of the time, Pallas kernels for 0%

commit v1 on v0

--- a/solution.py
+++ b/solution.py
@@ -4,6 +4,19 @@
 from jax.sharding import PartitionSpec as P
 
 LOSS_SCALE = 32768
+
+
+def collect(value, axis, dim):
+    ways = lax.axis_size(axis)
+    up = [(d, (d + 1) % ways) for d in range(ways)]
+    down = [(d, (d - 1) % ways) for d in range(ways)]
+    earlier, later = ([value], [value])
+    for _ in range(ways // 2):
+        earlier.append(lax.ppermute(earlier[-1], axis, up))
+    for _ in range((ways - 1) // 2):
+        later.append(lax.ppermute(later[-1], axis, down))
+    line = jnp.concatenate([*earlier[::-1], *later[1:]], axis=dim)
+    return jnp.roll(line, (lax.axis_index(axis) - ways // 2) * value.shape[dim], axis=dim)
 
 
 def body(cotangent, hidden, gates, expert_ids, group_counts, w_down):
@@ -41,10 +54,7 @@
     hid_four = hid_recv.reshape(n_exp, exp_dev, most, ffw)
     gate_three = gate_recv.reshape(n_exp, exp_dev, most).astype(jnp.float32)
     proj = jnp.einsum(
-        "sjmd,jfd->sjmf",
-        dy_four,
-        lax.all_gather(w_down, "grp", axis=1, tiled=True),
-        preferred_element_type=jnp.float32,
+        "sjmd,jfd->sjmf", dy_four, collect(w_down, "grp", 1), preferred_element_type=jnp.float32
     )
     dh_rows = (gate_three[..., None] * proj).astype(jnp.bfloat16)
     inner = jnp.sum(hid_four.astype(jnp.float32) * proj, axis=3).astype(jnp.bfloat16)

time: 502 us -> 539 us (1.074)
  blocking collectives: 15.4 us -> 68.1 us
  waiting for transfers between devices: 392 us -> 341 us
  local copies, waits for them, and re-layouts: 34.2 us -> 59.9 us
    all_gather x1 -> x0, waiting for transfers between devices: 83.1 us -> none  [body(): lax.all_gather(w_down, 'grp', axis=1, tiled=True)]
    psum x1, blocking collectives: 15.4 us -> 68.1 us  [body(): total = lax.psum(count.astype(jnp.float32), 'grp')]
    ppermute x0 -> x3, waiting for transfers between devices: none -> 48.2 us  [the longest x2 48.2 us: collect(): earlier.append(lax.ppermute(earlier[-1], axis, up))]
    unnamed x18 -> x23, local copies, waits for them, and re-layouts: 5.58 us -> 24.3 us
    all_to_all x1, waiting for transfers between devices: 15.5 us -> 0.01 us  [body(): lax.all_to_all(hid_buf, 'exp', split_axis=0, concat_axis=0, tiled=True)]
    unnamed x3 -> x2, waiting for transfers between devices: 262 us -> 260 us
  transfers between devices with their start and end apart: 7 -> 9, of which waited for: 6 -> 5; matrix products, arithmetic and copies ran while one was open for 7% -> 12% of each run, Pallas kernels for 0% -> 0%
where the time goes in v1:
time: 539 us
  waiting for transfers between devices  341 us (63%)
  blocking collectives  68.1 us (13%)
  local copies, waits for them, and re-layouts  59.9 us (11%)
  starting transfers between devices  25.5 us (5%)
  matrix products  20.6 us (4%)
  between operations  16.2 us (3%)
  other arithmetic  7.14 us (1%)
    unnamed x2, waiting for transfers between devices  260 us
    psum x1, blocking collectives, body(): total = lax.psum(count.astype(jnp.float32), 'grp')  68.1 us
    ppermute x2, waiting for transfers between devices, collect(): earlier.append(lax.ppermute(earlier[-1], axis, up))  48.2 us
    unnamed x23, local copies, waits for them, and re-layouts  24.3 us
    all_to_all x1, waiting for transfers between devices, body(): lax.all_to_all(dh_rows.reshape(n_exp, exp_dev * most, ffw), 'exp', split_...  19.2 us
    all_to_all x1, waiting for transfers between devices, body(): lax.all_to_all(dy_buf, 'exp', split_axis=0, concat_axis=0, tiled=True)  10.9 us
  transfers between devices with their start and end apart: 9, of which 5 were waited for; matrix products, arithmetic and copies ran while one was open for 12% of the time, Pallas kernels for 0%

profile of v1, /device:TPU:0, one launch (start us, length us, event | category | flops | bytes accessed | tf_op | source)
XLA Modules:
  0.0 538.6 jit_solution(13829810589064458386)
XLA Ops:
  7.2 3.1 collective-permute-start
  10.2 2.1 collective-permute-start.2
  13.2 48.2 %collective-permute-done = bf16[2,360,1440]{2,1,0:T(8,128)(2,1)S(1)} collective-permute-done((bf16[2,360,1440]{2,1,0:T(8,128)(2,1)}, bf16[2,360,1440]{2,1,0:T(8,128)(2,1)S(1)}, u32[]{:S(2)}, u32[]{:S(2)}) %collective-permute-start) | collective-permute-done | bytes 2073632 | tf_op jit(solution)/shard_map/ppermute | solution.py:15
  65.6 3.8 scatter_custom_fusion
  70.1 4.0 all-to-all-start
  74.0 3.9 copy.55
  77.9 3.7 reshape.220
  81.7 5.3 scatter_custom_fusion.2
  87.0 4.5 all-to-all-start.3
  91.4 68.1 %psum.7 = f32[]{:T(128)} all-reduce(f32[]{:T(128)S(6)} %convert_element_type.90), channel_id=1, replica_groups=mesh['grp'=4,'exp'=8] {'grp'}, use_global_device_ids=true, to_apply=%region_7.8 | all-reduce | flops 1 | bytes 8 | tf_op jit(solution)/shard_map/psum | solution.py:34
  159.7 9.6 %scatter_custom_fusion.1 = bf16[640,1440]{1,0:T(8,128)(2,1)} fusion(s32[512]{0:T(512)S(1)} %bitcast.59, bf16[128,1440]{1,0:T(8,128)(2,1)S(1)} %copy.52, s32[1024]{0:T(1024)S(1)} %pad_clamp_fusion.1, bf16[]{:T(256)} %constant.52.clone.1), kind=kCustom, calls=%fused_computation.19 | custom fusion | bytes 1843202 | tf_op jit(solution)/shard_map/scatter | solution.py:42
  170.2 3.2 constant_dynamic-update-slice_fusion.7
  173.3 1.6 constant_dynamic-update-slice_fusion.6
  174.9 4.5 all-to-all-start.1
  179.7 1.5 constant_dynamic-update-slice_fusion.5
  181.2 3.1 constant_dynamic-update-slice_fusion.4
  184.3 3.3 constant_dynamic-update-slice_fusion.3
  187.6 1.5 constant_dynamic-update-slice_fusion.2
  189.1 1.5 constant_dynamic-update-slice_fusion.1
  190.6 3.1 constant_dynamic-update-slice_fusion
  193.8 10.9 %all-to-all-done.1 = bf16[8,80,1440]{2,1,0:T(8,128)(2,1)} async-done(((bf16[8,80,1440]{2,1,0:T(8,128)(2,1)}), bf16[8,80,1440]{2,1,0:T(8,128)(2,1)}, u32[]{:S(2)}, u32[]{:S(2)}) %all-to-all-start.1) | async-done | bytes 1843232 | tf_op jit(solution)/shard_map/all_to_all | solution.py:49
  204.7 10.3 %fusion.5 = (bf16[8,2,40]{2,0,1:T(8,128)(2,1)S(1)}, bf16[8,2,40,1440]{3,2,0,1:T(8,128)(2,1)S(1)}, bf16[8,2,40,1440]{3,2,0,1:T(8,128)(2,1)}) fusion(bf16[8,2,40,1440]{3,2,1,0:T(8,128)(2,1)} %bitcast.13, f32[8,2,40]{2,0,1:T(8,128)S(1)} %copy.51, bf16[8,2,40,1440]{3,2,1,0:T(8,128)(2,1)} %bitcast.8, ...), kind=kOutput, calls=%fused_computation.14 | convolution fusion | flops 2661580288 | bytes 18435844 | tf_op jit(solution)/shard_map/sjmd,jfd->sjmf/dot_general | solution.py:56
  215.0 10.3 %fusion = bf16[2,1440,1440]{2,1,0:T(8,128)(2,1)} fusion(bf16[8,2,40,1440]{3,2,1,0:T(8,128)(2,1)} %bitcast.13, f32[]{:T(128)S(6)} %div.13, bf16[8,2,40,1440]{3,2,0,1:T(8,128)(2,1)} %get-tuple-element.17), kind=kOutput, calls=%fused_computation.7 | convolution fusion | flops 2662502400 | bytes 11980804 | tf_op jit(solution)/shard_map/sjmf,sjmd->jfd/dot_general | solution.py:63
  226.0 3.3 all-to-all-start.4
  230.8 3.0 all-to-all-done.4
  233.8 3.9 all-to-all-start.2
  239.1 3.5 gather_fusion.1
  243.5 19.2 %all-to-all-done.2 = bf16[8,80,1440]{2,1,0:T(8,128)(2,1)S(1)} async-done(((bf16[8,80,1440]{2,1,0:T(8,128)(2,1)}), bf16[8,80,1440]{2,1,0:T(8,128)(2,1)S(1)}, u32[]{:S(2)}, u32[]{:S(2)}) %all-to-all-start.2) | async-done | bytes 1843232 | tf_op jit(solution)/shard_map/all_to_all | solution.py:69
  262.6 2.1 gather_fusion
  265.2 2.4 copy.61
  267.6 259.8 %all-reduce.3.cloned.1.call-done = bf16[2,1440,1440]{2,1,0:T(8,128)(2,1)} async-done(((bf16[2,1440,1440]{2,1,0:T(8,128)(2,1)}), bf16[2,1440,1440]{2,1,0:T(8,128)(2,1)}) %all-reduce.3.cloned.1.call-update) | async-done | bytes 8294416
  527.5 4.3 dynamic-slice_convert_fusion
  (52 shorter events, 9.8 us)
Async XLA Ops:
  7.2 54.3 %collective-permute-start = (bf16[2,360,1440]{2,1,0:T(8,128)(2,1)}, bf16[2,360,1440]{2,1,0:T(8,128)(2,1)S(1)}, u32[]{:S(2)}, u32[]{:S(2)}) collective-permute-start(bf16[2,360,1440]{2,1,0:T(8,128)(2,1)} %param.11), channel_id=1, source_target_pairs={{0,8},{8,16},{16,24},{24,0},{1,9},{9,17},{17,25},{25,1},{2,10},{10... | collective-permute-start | bytes 6220808 | tf_op jit(solution)/shard_map/ppermute | solution.py:15
  10.2 171.0 %collective-permute-start.2 = (bf16[2,360,1440]{2,1,0:T(8,128)(2,1)}, bf16[2,360,1440]{2,1,0:T(8,128)(2,1)}, u32[]{:S(2)}, u32[]{:S(2)}) collective-permute-start(bf16[2,360,1440]{2,1,0:T(8,128)(2,1)} %param.11), channel_id=1, source_target_pairs={{0,24},{8,0},{16,8},{24,16},{1,25},{9,1},{17,9},{25,17},{2,26},{10... | collective-permute-start | bytes 6220808 | tf_op jit(solution)/shard_map/ppermute | solution.py:17
  61.4 111.9 %copy-start.1 = (bf16[2,360,1440]{2,1,0:T(8,128)(2,1)}, bf16[2,360,1440]{2,1,0:T(8,128)(2,1)S(1)}, u32[]{:S(2)}) copy-start(bf16[2,360,1440]{2,1,0:T(8,128)(2,1)S(1)} %collective-permute-done) | copy-start | bytes 6220804
  61.4 108.7 %collective-permute-start.1 = (bf16[2,360,1440]{2,1,0:T(8,128)(2,1)S(1)}, bf16[2,360,1440]{2,1,0:T(8,128)(2,1)}, u32[]{:S(2)}, u32[]{:S(2)}) collective-permute-start(bf16[2,360,1440]{2,1,0:T(8,128)(2,1)S(1)} %collective-permute-done), channel_id=1, source_target_pairs={{0,8},{8,16},{16,24},{24,0},{1,9},{9,17},{17,25},{25,1},{2,10},{10... | collective-permute-start | bytes 6220808 | tf_op jit(solution)/shard_map/ppermute | solution.py:15
  70.1 16.9 %all-to-all-start = ((bf16[8,1,80]{2,1,0:T(2,128)(2,1)}), bf16[8,1,80]{2,1,0:T(2,128)(2,1)S(1)}, u32[]{:S(2)}, u32[]{:S(2)}) async-start(bf16[8,1,80]{2,1,0:T(2,128)(2,1)} %all_to_all.25), calls=%async_computation | async-start | bytes 8192 | tf_op jit(solution)/shard_map/all_to_all | solution.py:50
  87.0 72.5 %copy-start.3 = (bf16[128,1440]{0,1:T(8,128)(2,1)S(1)}, bf16[128,1440]{0,1:T(8,128)(2,1)}, u32[]{:S(2)}) copy-start(bf16[128,1440]{0,1:T(8,128)(2,1)} %param.6) | copy-start | bytes 1105924
  87.0 88.0 %all-to-all-start.3 = ((bf16[8,80,1440]{2,1,0:T(8,128)(2,1)}), bf16[8,80,1440]{2,1,0:T(8,128)(2,1)}, u32[]{:S(2)}, u32[]{:S(2)}) async-start(bf16[8,80,1440]{2,1,0:T(8,128)(2,1)} %bitcast.54), calls=%async_computation.3 | async-start | bytes 3932160 | tf_op jit(solution)/shard_map/all_to_all | solution.py:52
  174.9 4.8 copy-start
  174.9 29.7 %all-to-all-start.1 = ((bf16[8,80,1440]{2,1,0:T(8,128)(2,1)}), bf16[8,80,1440]{2,1,0:T(8,128)(2,1)}, u32[]{:S(2)}, u32[]{:S(2)}) async-start(bf16[8,80,1440]{2,1,0:T(8,128)(2,1)} %bitcast.55), calls=%async_computation.1 | async-start | bytes 3932160 | tf_op jit(solution)/shard_map/all_to_all | solution.py:49
  179.4 348.0 %all-reduce.3.cloned.1.call-start = ((), (), s32[]{:S(2)}) async-start(), calls=%async_computation.5 | async-start | bytes 17694720
  184.3 3.3 copy-start.2
  226.0 7.8 %all-to-all-start.4 = ((bf16[8,1,80]{2,1,0:T(2,128)(2,1)}), bf16[8,1,80]{2,1,0:T(2,128)(2,1)S(1)}, u32[]{:S(2)}, u32[]{:S(2)}) async-start(bf16[8,1,80]{2,1,0:T(2,128)(2,1)} %convert_element_type.95), calls=%async_computation.4 | async-start | bytes 8192 | tf_op jit(solution)/shard_map/all_to_all | solution.py:76
  230.8 6.9 %copy-start.4 = (u32[32]{0:T(128)S(1)}, u32[32]{0:T(128)}, u32[]{:S(2)}) copy-start(u32[32]{0:T(128)} %constant.73) | copy-start | bytes 388
  233.8 28.8 %all-to-all-start.2 = ((bf16[8,80,1440]{2,1,0:T(8,128)(2,1)}), bf16[8,80,1440]{2,1,0:T(8,128)(2,1)S(1)}, u32[]{:S(2)}, u32[]{:S(2)}) async-start(bf16[8,80,1440]{2,1,0:T(8,128)(2,1)} %bitcast.56), calls=%async_computation.2 | async-start | bytes 3932160 | tf_op jit(solution)/shard_map/all_to_all | solution.py:69
Sparse Core Ops, SparseCore 0:
  225.4 301.9 all-reduce.2
